TPU v7x, 512 devices: a whole 4x4x16 slice. The times are simulated.
512 devices in a mesh: dp: 32 (over y, x, core), wide: 16 (over z).
Axes of the slice: x: 4, y: 4, z: 16, core: 2. Of those that a mesh axis runs over, the one named last changes fastest.
Arguments:
- trunk_out: bfloat16 [16384, 1024], P('dp'), may hold values from -6 to 6
- projection: bfloat16 [1024, 4096], P(None, 'wide'), may hold values from -0.1875 to 0.1875
- transform: bfloat16 [4096, 4096], P('wide'), may hold values from -0.125 to 0.125
- block_mask: int32 [32, 32], P('wide'), may hold values from 0 to 1, as said below
- old_index: bfloat16 [16384, 4096], P('dp', 'wide'), may hold values from -6 to 6
- doc_ids: int32 [16384, 4], P('dp'), may hold values from 0 to 16383, as said below
- labels: int32 [16384, 4], P('dp'), may hold values 0 or 1
Outputs:
- new_embed: bfloat16 [16384, 4096], P('dp', 'wide')
- pair_loss: float32 [16384, 4], P('dp')
- trunk_grad: bfloat16 [16384, 4096], P('dp', 'wide')
Inputs may be any that keep to these rules, and one draw needn't show every extreme that they name: `doc_ids`: in each aligned block of 512 rows, no shard id // 512 is named more than 128 times, and one shard is named exactly 128 times. `block_mask`: each block row has 4 to 24 nonzero entries, and some block row has exactly 24.
All inputs are finite; a program needn't handle non-finite values. No bound on the sum of `labels` on one device may be relied on, other than what follows from the above.
Results may differ from a plain program's by a relative error of at most 0.015.
Values may be sent and summed in bfloat16 or wider, within the bound.
No kernel may reach another device: no remote copies, remote signals or barrier semaphores. Data moves between devices by JAX's collectives and lax.ppermute only.
A program may use at most 128 MiB of HBM per device.

v0:
```python
import math
import jax
import jax.numpy as jnp
from jax import lax
from jax.sharding import PartitionSpec as P

E = 4096
K = 4
CAP = 128


def local(n_dp, trunk_out, projection, transform, block_mask, old_index, doc_ids, labels):
    rows, dmodel = trunk_out.shape
    e_local, width = transform.shape
    local_blocks, nblocks = block_mask.shape
    side = e_local // local_blocks
    doc_shard = old_index.shape[0]
    blocks = transform.reshape(local_blocks, side, nblocks, side)
    masked = (blocks * block_mask[:, None, :, None].astype(jnp.bfloat16)).reshape(e_local, width)
    chunk = dmodel // n_dp
    me = lax.axis_index("dp")
    proj_rows = lax.dynamic_slice_in_dim(projection, me * chunk, chunk, 0)
    w_part = jnp.dot(proj_rows, masked, preferred_element_type=jnp.float32)
    w_blk = lax.psum_scatter(w_part, "wide", scatter_dimension=1, tiled=True)
    w_cols = lax.all_gather(w_blk.astype(jnp.bfloat16), "dp", axis=0, tiled=True)
    new = jnp.dot(trunk_out, w_cols, preferred_element_type=jnp.float32)
    flat = doc_ids.reshape(-1)
    owner = flat // doc_shard
    loc = flat - owner * doc_shard
    onehot = (owner[:, None] == jnp.arange(n_dp, dtype=jnp.int32)[None, :]).astype(jnp.int32)
    before = jnp.cumsum(onehot, axis=0) - onehot
    rank = jnp.sum(before * onehot, axis=1)
    slot = owner * CAP + rank
    req = jnp.zeros((n_dp * CAP,), jnp.int32).at[slot].set(loc, unique_indices=True)
    asked = lax.all_to_all(req.reshape(n_dp, CAP), "dp", 0, 0, tiled=True)
    served = old_index[asked.reshape(-1)].reshape(n_dp, CAP, e_local)
    back = lax.all_to_all(served, "dp", 0, 0, tiled=True).reshape(n_dp * CAP, e_local)
    old_vec = back[slot].reshape(rows, K, e_local)
    old_wide = old_vec.astype(jnp.float32)
    scale = 1.0 / math.sqrt(E)
    partial_scores = jnp.einsum("re,rke->rk", new, old_wide)
    score = lax.psum(partial_scores, "wide") * scale
    sign = 2.0 * labels.astype(jnp.float32) - 1.0
    pair_loss = jax.nn.softplus(-sign * score)
    dscore = -sign * jax.nn.sigmoid(-sign * score)
    grad_local = (jnp.einsum("rk,rke->re", dscore, old_wide) * scale).astype(jnp.bfloat16)
    grad_full = lax.all_gather(grad_local, "wide", axis=1, tiled=True)
    trunk_grad = lax.dot_general(
        grad_full, masked, (((1,), (1,)), ((), ())), preferred_element_type=jnp.float32
    )
    return (new.astype(jnp.bfloat16), pair_loss, trunk_grad.astype(jnp.bfloat16))


def solution(mesh):
    n_dp = mesh.shape["dp"]
    return jax.shard_map(
        lambda *a: local(n_dp, *a),
        mesh=mesh,
        in_specs=(
            P("dp", None),
            P(None, "wide"),
            P("wide", None),
            P("wide", None),
            P("dp", "wide"),
            P("dp", None),
            P("dp", None),
        ),
        out_specs=(P("dp", "wide"), P("dp", None), P("dp", "wide")),
        check_vma=False,
    )
```

profile of v0, /device:TPU:2, one launch (start us, length us, event | category | flops | bytes accessed | tf_op | source)
XLA Modules:
  0.0 318.5 jit_solution(10625858685940429330)
XLA Ops:
  7.2 0.9 copy.11
  8.7 9.1 %reduce-window.6 = s32[32,16,128]{2,1,0:T(8,128)S(1)} reduce-window(s32[32,16,128]{2,1,0:T(8,128)S(1)} %fusion.5, s32[]{:T(128)} %constant.20.clone.1), window={size=1x1x128 pad=0_0x0_0x127_0}, to_apply=%region_1.2 | reduce-window | flops 8323072 | bytes 524292 | tf_op jit(solution)/shard_map/reduce-window
  18.7 8.1 %scatter_custom_fusion = s32[4096]{0:T(1024)S(1)} fusion(s32[2048]{0:T(1024)S(1)} %bitcast.60, s32[2048]{0:T(1024)S(1)} %get-tuple-element.9, s32[]{:T(128)} %constant.20.clone.1), kind=kCustom, calls=%fused_computation.42 | custom fusion | bytes 16388 | tf_op jit(solution)/shard_map/scatter | solution.py:34
  26.7 14.8 %all_to_all.14 = s32[32,1,128]{2,1,0:T(1,128)S(1)} all-to-all(s32[32,1,128]{2,1,0:T(1,128)S(1)} %bitcast.57), channel_id=1, replica_groups=mesh['dp'=32,'wide'=16] {'dp'}, dimensions={0} | all-to-all | bytes 32768 | tf_op jit(solution)/shard_map/all_to_all | solution.py:35
  41.6 16.9 %gather_fusion = bf16[4096,256]{1,0:T(8,128)(2,1)} fusion(bf16[512,256]{1,0:T(8,128)(2,1)S(1)} %copy-done.1, s32[4096]{0:T(1024)S(1)} %broadcast_clamp_fusion), kind=kCustom, calls=%fused_computation | custom fusion | bytes 4210688 | tf_op jit(solution)/shard_map/gather | solution.py:36
  58.5 5.2 %all-to-all-start.1 = ((bf16[32,128,256]{2,1,0:T(8,128)(2,1)}), bf16[32,128,256]{2,1,0:T(8,128)(2,1)S(1)}, u32[]{:S(2)}, u32[]{:S(2)}) async-start(bf16[32,128,256]{2,1,0:T(8,128)(2,1)} %bitcast.53), calls=%async_computation.2 | async-start | bytes 4194304 | tf_op jit(solution)/shard_map/all_to_all | solution.py:37
  64.2 1.3 copy-done.2
  66.1 2.4 fusion
  68.5 72.4 %reduce-scatter.2.cloned.1.call-done = f32[32,256]{1,0:T(8,128)} async-done(((f32[32,4096]{1,0:T(8,128)}), f32[32,256]{1,0:T(8,128)}) %reduce-scatter.2.cloned.1.call-update) | async-done | bytes 32784 | tf_op jit(solution)/shard_map/reduce_scatter | solution.py:24
  140.9 0.8 convert_element_type.28
  141.7 24.5 %all_gather.6 = bf16[1024,256]{1,0:T(8,128)(2,1)S(1)} all-gather(bf16[32,256]{1,0:T(8,128)(2,1)S(1)} %convert_element_type.28), channel_id=1, replica_groups=mesh['dp'=32,'wide'=16] {'dp'}, dimensions={0}, use_global_device_ids=true | all-gather | bytes 540672 | tf_op jit(solution)/shard_map/all_gather | solution.py:25
  166.2 1.3 fusion.15
  167.5 2.0 copy.26
  169.5 9.0 %gather_fusion.1 = bf16[2048,256]{1,0:T(8,128)(2,1)} fusion(bf16[4096,256]{1,0:T(8,128)(2,1)S(1)} %bitcast.50, s32[2048]{0:T(1024)S(1)} %broadcast_clamp_fusion.1), kind=kCustom, calls=%fused_computation.1 | custom fusion | bytes 2105344 | tf_op jit(solution)/shard_map/gather | solution.py:38
  178.5 1.4 reshape.188
  179.9 0.6 multiply_reduce_fusion
  180.7 28.9 %psum.7 = f32[512,4]{0,1:T(4,128)S(1)} all-reduce(f32[512,4]{0,1:T(4,128)S(1)} %copy.21), channel_id=1, replica_groups=mesh['dp'=32,'wide'=16] {'wide'}, use_global_device_ids=true, to_apply=%region_5.6 | all-reduce | flops 2048 | bytes 16384 | tf_op jit(solution)/shard_map/psum | solution.py:42
  209.6 0.9 copy.22
  210.5 2.1 fusion.16
  212.7 0.7 fusion.1
  213.4 0.8 copy.16
  214.3 0.6 compare_select_fusion.2
  214.9 91.9 %all-gather.2.cloned.1.call-done = bf16[512,4096]{1,0:T(8,128)(2,1)} async-done(((bf16[512,256]{1,0:T(8,128)(2,1)}), bf16[512,4096]{1,0:T(8,128)(2,1)}) %all-gather.2.cloned.1.call-update) | async-done | bytes 4194320 | tf_op jit(solution)/shard_map/all_gather | solution.py:47
  306.8 4.9 %convolution_convert_fusion = bf16[512,256]{1,0:T(8,128)(2,1)} fusion(bf16[512,4096]{1,0:T(8,128)(2,1)} %all-gather.2.cloned.1.call-done, bf16[256,4096]{1,0:T(8,128)(2,1)} %param.9, bf16[32,8,32,128]{3,2,1,0:T(8,128)(2,1)S(1)} %bitcast.52), kind=kOutput, calls=%fused_computation.6 | convolution fusion | flops 1074921472 | bytes 8650752 | tf_op jit(solution)/shard_map/dot_general | solution.py:48
  (41 shorter events, 2.6 us)
Async XLA Ops:
  7.2 159.0 %copy-start = (bf16[512,1024]{1,0:T(8,128)(2,1)S(1)}, bf16[512,1024]{1,0:T(8,128)(2,1)}, u32[]{:S(2)}) copy-start(bf16[512,1024]{1,0:T(8,128)(2,1)} %param.7) | copy-start | bytes 3145732
  7.2 34.4 %copy-start.1 = (bf16[512,256]{1,0:T(8,128)(2,1)S(1)}, bf16[512,256]{1,0:T(8,128)(2,1)}, u32[]{:S(2)}) copy-start(bf16[512,256]{1,0:T(8,128)(2,1)} %param.11) | copy-start | bytes 786436
  58.5 5.3 %copy-start.8 = (s32[2,32]{1,0:T(2,128)S(1)}, s32[2,32]{1,0:T(2,128)}, u32[]{:S(2)}) copy-start(s32[2,32]{1,0:T(2,128)} %param.10) | copy-start | bytes 772
  58.5 111.0 %all-to-all-start.1 = ((bf16[32,128,256]{2,1,0:T(8,128)(2,1)}), bf16[32,128,256]{2,1,0:T(8,128)(2,1)S(1)}, u32[]{:S(2)}, u32[]{:S(2)}) async-start(bf16[32,128,256]{2,1,0:T(8,128)(2,1)} %bitcast.53), calls=%async_computation.2 | async-start | bytes 4194304 | tf_op jit(solution)/shard_map/all_to_all | solution.py:37
  63.8 77.2 %reduce-scatter.2.cloned.1.call-start = ((), (), s32[]{:S(2)}) async-start(), calls=%async_computation.3 | async-start | bytes 557056 | tf_op jit(solution)/shard_map/reduce_scatter | solution.py:24
  63.8 2.2 copy-start.5
  64.2 1.3 copy-start.2
  68.5 238.3 %all-gather.2.cloned.1.call-start = ((), (), s32[]{:S(2)}) async-start(), calls=%async_computation.4 | async-start | bytes 4456448 | tf_op jit(solution)/shard_map/all_gather | solution.py:47
  178.5 1.4 copy-start.6
  178.5 31.1 %copy-start.7 = (s32[512,4]{0,1:T(4,128)S(1)}, s32[512,4]{0,1:T(4,128)}, u32[]{:S(2)}) copy-start(s32[512,4]{0,1:T(4,128)} %param.13) | copy-start | bytes 24580
  179.9 29.7 %copy-start.4 = (bf16[512,4,256]{2,1,0:T(4,128)(2,1)}, bf16[512,4,256]{2,1,0:T(4,128)(2,1)S(1)}, u32[]{:S(2)}) copy-start(bf16[512,4,256]{2,1,0:T(4,128)(2,1)S(1)} %reshape.188) | copy-start | bytes 3145732
  210.5 96.3 %copy-start.3 = (bf16[2,128,32,128]{3,2,1,0:T(8,128)(2,1)S(1)}, bf16[2,128,32,128]{3,2,1,0:T(8,128)(2,1)}, u32[]{:S(2)}) copy-start(bf16[2,128,32,128]{3,2,1,0:T(8,128)(2,1)} %copy-done.2) | copy-start | bytes 6291460
Sparse Core Ops, SparseCore 0:
  68.6 72.2 reduce-scatter.1
  213.6 93.1 all-gather.1
where the time goes:
time: 319 us
  waiting for transfers between devices  164 us (51%)
  blocking collectives  68.1 us (21%)
  local copies, waits for them, and re-layouts  43.3 us (14%)
  between operations  14.3 us (4%)
  other arithmetic  12.4 us (4%)
  matrix products  10.7 us (3%)
  starting transfers between devices  5.33 us (2%)
    all_gather x1, waiting for transfers between devices, local(): grad_full = lax.all_gather(grad_local, 'wide', axis=1, tiled=True)  91.9 us
    reduce_scatter x1, waiting for transfers between devices, local(): w_blk = lax.psum_scatter(w_part, 'wide', scatter_dimension=1, tiled=True)  72.4 us
    psum x1, blocking collectives, local(): score = lax.psum(partial_scores, 'wide') * scale  28.9 us
    all_gather x1, blocking collectives, local(): lax.all_gather(w_blk.astype(jnp.bfloat16), 'dp', axis=0, tiled=True)  24.5 us
    gather x1, local copies, waits for them, and re-layouts, local(): served = old_index[asked.reshape(-1)].reshape(n_dp, CAP, e_local)  16.9 us
    all_to_all x1, blocking collectives, local(): asked = lax.all_to_all(req.reshape(n_dp, CAP), 'dp', 0, 0, tiled=True)  14.8 us
    another operation x3, other arithmetic  9.41 us
    gather x1, local copies, waits for them, and re-layouts, local(): old_vec = back[slot].reshape(rows, K, e_local)  9 us
  transfers between devices with their start and end apart: 3, of which 2 were waited for; matrix products, arithmetic and copies ran while one was open for 3% of the time, Pallas kernels for 0%

commit v1 on v0

--- a/solution.py
+++ b/solution.py
@@ -44,7 +44,9 @@
     pair_loss = jax.nn.softplus(-sign * score)
     dscore = -sign * jax.nn.sigmoid(-sign * score)
     grad_local = (jnp.einsum("rk,rke->re", dscore, old_wide) * scale).astype(jnp.bfloat16)
-    grad_full = lax.all_gather(grad_local, "wide", axis=1, tiled=True)
+    grad_full = jnp.concatenate(
+        lax.all_to_all(jnp.stack([grad_local] * lax.axis_size("wide")), "wide", 0, 0), axis=1
+    )
     trunk_grad = lax.dot_general(
         grad_full, masked, (((1,), (1,)), ((), ())), preferred_element_type=jnp.float32
     )

time: 319 us -> 418 us (1.31)
  waiting for transfers between devices: 164 us -> 251 us
  starting transfers between devices: 5.33 us -> 15.4 us
    all_to_all x0 -> x1, waiting for transfers between devices: none -> 179 us  [local(): lax.all_to_all(jnp.stack([grad_local] * lax.axis_size('wide')), 'wide', 0...]
    all_gather x1 -> x0, waiting for transfers between devices: 91.9 us -> none  [local(): grad_full = lax.all_gather(grad_local, 'wide', axis=1, tiled=True)]
    all_to_all x0 -> x1, starting transfers between devices: none -> 10.1 us  [local(): lax.all_to_all(jnp.stack([grad_local] * lax.axis_size('wide')), 'wide', 0...]
  transfers between devices with their start and end apart: 3 -> 3, of which waited for: 2 -> 2; matrix products, arithmetic and copies ran while one was open for 3% -> 2% of each run, Pallas kernels for 0% -> 0%
where the time goes in v1:
time: 418 us; the launch traced here: 417 us
  waiting for transfers between devices  251 us (60%)
  blocking collectives  68.1 us (16%)
  local copies, waits for them, and re-layouts  45.1 us (11%)
  starting transfers between devices  15.4 us (4%)
  other arithmetic  14.6 us (3%)
  between operations  14.3 us (3%)
  matrix products  8.82 us (2%)
    all_to_all x1, waiting for transfers between devices, local(): lax.all_to_all(jnp.stack([grad_local] * lax.axis_size('wide')), 'wide', 0...  179 us
    reduce_scatter x1, waiting for transfers between devices, local(): w_blk = lax.psum_scatter(w_part, 'wide', scatter_dimension=1, tiled=True)  72.4 us
    psum x1, blocking collectives, local(): score = lax.psum(partial_scores, 'wide') * scale  28.9 us
    all_gather x1, blocking collectives, local(): lax.all_gather(w_blk.astype(jnp.bfloat16), 'dp', axis=0, tiled=True)  24.5 us
    gather x1, local copies, waits for them, and re-layouts, local(): served = old_index[asked.reshape(-1)].reshape(n_dp, CAP, e_local)  16.9 us
    all_to_all x1, blocking collectives, local(): asked = lax.all_to_all(req.reshape(n_dp, CAP), 'dp', 0, 0, tiled=True)  14.8 us
    all_to_all x1, starting transfers between devices, local(): lax.all_to_all(jnp.stack([grad_local] * lax.axis_size('wide')), 'wide', 0...  10.1 us
    another operation x3, other arithmetic  9.41 us
  transfers between devices with their start and end apart: 3, of which 2 were waited for; matrix products, arithmetic and copies ran while one was open for 2% of the time, Pallas kernels for 0%

profile of v1, /device:TPU:2, one launch (start us, length us, event | category | flops | bytes accessed | tf_op | source)
XLA Modules:
  0.0 417.3 jit_solution(782373337876737471)
XLA Ops:
  7.2 0.9 copy.11
  8.7 9.1 %reduce-window.6 = s32[32,16,128]{2,1,0:T(8,128)S(1)} reduce-window(s32[32,16,128]{2,1,0:T(8,128)S(1)} %fusion.4, s32[]{:T(128)} %constant.20.clone.1), window={size=1x1x128 pad=0_0x0_0x127_0}, to_apply=%region_1.2 | reduce-window | flops 8323072 | bytes 524292 | tf_op jit(solution)/shard_map/reduce-window
  18.7 8.1 %scatter_custom_fusion = s32[4096]{0:T(1024)S(1)} fusion(s32[2048]{0:T(1024)S(1)} %bitcast.55, s32[2048]{0:T(1024)S(1)} %get-tuple-element.11, s32[]{:T(128)} %constant.20.clone.1), kind=kCustom, calls=%fused_computation.42 | custom fusion | bytes 16388 | tf_op jit(solution)/shard_map/scatter | solution.py:34
  26.7 14.8 %all_to_all.19 = s32[32,1,128]{2,1,0:T(1,128)S(1)} all-to-all(s32[32,1,128]{2,1,0:T(1,128)S(1)} %bitcast.52), channel_id=1, replica_groups=mesh['dp'=32,'wide'=16] {'dp'}, dimensions={0} | all-to-all | bytes 32768 | tf_op jit(solution)/shard_map/all_to_all | solution.py:35
  41.6 16.9 %gather_fusion = bf16[4096,256]{1,0:T(8,128)(2,1)} fusion(bf16[512,256]{1,0:T(8,128)(2,1)S(1)} %copy-done.1, s32[4096]{0:T(1024)S(1)} %broadcast_clamp_fusion), kind=kCustom, calls=%fused_computation | custom fusion | bytes 4210688 | tf_op jit(solution)/shard_map/gather | solution.py:36
  58.5 5.2 %all-to-all-start.1 = ((bf16[32,128,256]{2,1,0:T(8,128)(2,1)}), bf16[32,128,256]{2,1,0:T(8,128)(2,1)S(1)}, u32[]{:S(2)}, u32[]{:S(2)}) async-start(bf16[32,128,256]{2,1,0:T(8,128)(2,1)} %bitcast.48), calls=%async_computation.2 | async-start | bytes 4194304 | tf_op jit(solution)/shard_map/all_to_all | solution.py:37
  64.2 1.4 copy-done.2
  66.1 2.4 fusion
  68.5 72.4 %reduce-scatter.2.cloned.1.call-done = f32[32,256]{1,0:T(8,128)} async-done(((f32[32,4096]{1,0:T(8,128)}), f32[32,256]{1,0:T(8,128)}) %reduce-scatter.2.cloned.1.call-update) | async-done | bytes 32784 | tf_op jit(solution)/shard_map/reduce_scatter | solution.py:24
  140.9 0.8 convert_element_type.28
  141.7 24.5 %all_gather.3 = bf16[1024,256]{1,0:T(8,128)(2,1)S(1)} all-gather(bf16[32,256]{1,0:T(8,128)(2,1)S(1)} %convert_element_type.28), channel_id=1, replica_groups=mesh['dp'=32,'wide'=16] {'dp'}, dimensions={0}, use_global_device_ids=true | all-gather | bytes 540672 | tf_op jit(solution)/shard_map/all_gather | solution.py:25
  166.2 1.3 fusion.13
  167.5 2.0 copy.28
  169.5 9.0 %gather_fusion.1 = bf16[2048,256]{1,0:T(8,128)(2,1)} fusion(bf16[4096,256]{1,0:T(8,128)(2,1)S(1)} %bitcast.45, s32[2048]{0:T(1024)S(1)} %broadcast_clamp_fusion.1), kind=kCustom, calls=%fused_computation.1 | custom fusion | bytes 2105344 | tf_op jit(solution)/shard_map/gather | solution.py:38
  178.5 1.4 reshape.196
  179.9 0.6 multiply_reduce_fusion.1
  180.7 28.9 %psum.7 = f32[512,4]{0,1:T(4,128)S(1)} all-reduce(f32[512,4]{0,1:T(4,128)S(1)} %copy.21), channel_id=1, replica_groups=mesh['dp'=32,'wide'=16] {'wide'}, use_global_device_ids=true, to_apply=%region_5.6 | all-reduce | flops 2048 | bytes 16384 | tf_op jit(solution)/shard_map/psum | solution.py:42
  209.6 0.6 divide_multiply_fusion
  210.3 2.9 multiply_reduce_fusion
  213.5 2.4 stack.2
  215.8 10.1 %all-to-all-start.2 = ((bf16[16,512,256]{1,2,0:T(8,128)(2,1)}), bf16[16,512,256]{1,2,0:T(8,128)(2,1)}, u32[]{:S(2)}, u32[]{:S(2)}) async-start(bf16[16,512,256]{1,2,0:T(8,128)(2,1)} %stack.2), calls=%async_computation.3 | async-start | bytes 8388608 | tf_op jit(solution)/shard_map/all_to_all | solution.py:48
  226.0 0.8 copy.16
  226.8 178.5 %all-to-all-done.2 = bf16[16,512,256]{1,2,0:T(8,128)(2,1)} async-done(((bf16[16,512,256]{1,2,0:T(8,128)(2,1)}), bf16[16,512,256]{1,2,0:T(8,128)(2,1)}, u32[]{:S(2)}, u32[]{:S(2)}) %all-to-all-start.2) | async-done | bytes 4194336 | tf_op jit(solution)/shard_map/all_to_all | solution.py:48
  405.3 5.1 %convolution_convert_fusion = bf16[512,256]{1,0:T(8,128)(2,1)} fusion(bf16[512,4096]{0,1:T(8,128)(2,1)} %bitcast.13, bf16[256,4096]{1,0:T(8,128)(2,1)} %param.9, bf16[32,8,32,128]{3,2,1,0:T(8,128)(2,1)S(1)} %bitcast.47), kind=kOutput, calls=%fused_computation.7 | convolution fusion | flops 1074921472 | bytes 8650752 | tf_op jit(solution)/shard_map/dot_general | solution.py:50
  (39 shorter events, 2.8 us)
Async XLA Ops:
  7.2 159.0 %copy-start = (bf16[512,1024]{1,0:T(8,128)(2,1)S(1)}, bf16[512,1024]{1,0:T(8,128)(2,1)}, u32[]{:S(2)}) copy-start(bf16[512,1024]{1,0:T(8,128)(2,1)} %param.7) | copy-start | bytes 3145732
  7.2 34.4 %copy-start.1 = (bf16[512,256]{1,0:T(8,128)(2,1)S(1)}, bf16[512,256]{1,0:T(8,128)(2,1)}, u32[]{:S(2)}) copy-start(bf16[512,256]{1,0:T(8,128)(2,1)} %param.11) | copy-start | bytes 786436
  58.5 5.3 %copy-start.7 = (s32[2,32]{1,0:T(2,128)S(1)}, s32[2,32]{1,0:T(2,128)}, u32[]{:S(2)}) copy-start(s32[2,32]{1,0:T(2,128)} %param.10) | copy-start | bytes 772
  58.5 111.0 %all-to-all-start.1 = ((bf16[32,128,256]{2,1,0:T(8,128)(2,1)}), bf16[32,128,256]{2,1,0:T(8,128)(2,1)S(1)}, u32[]{:S(2)}, u32[]{:S(2)}) async-start(bf16[32,128,256]{2,1,0:T(8,128)(2,1)} %bitcast.48), calls=%async_computation.2 | async-start | bytes 4194304 | tf_op jit(solution)/shard_map/all_to_all | solution.py:37
  63.8 77.2 %reduce-scatter.2.cloned.1.call-start = ((), (), s32[]{:S(2)}) async-start(), calls=%async_computation.4 | async-start | bytes 557056 | tf_op jit(solution)/shard_map/reduce_scatter | solution.py:24
  63.8 2.2 copy-start.4
  64.2 1.4 copy-start.2
  178.5 1.4 copy-start.5
  178.5 31.1 %copy-start.6 = (s32[512,4]{0,1:T(4,128)S(1)}, s32[512,4]{0,1:T(4,128)}, u32[]{:S(2)}) copy-start(s32[512,4]{0,1:T(4,128)} %param.13) | copy-start | bytes 24580
  215.8 189.5 %copy-start.3 = (bf16[2,128,32,128]{3,2,1,0:T(8,128)(2,1)S(1)}, bf16[2,128,32,128]{3,2,1,0:T(8,128)(2,1)}, u32[]{:S(2)}) copy-start(bf16[2,128,32,128]{3,2,1,0:T(8,128)(2,1)} %copy-done.2) | copy-start | bytes 6291460
  215.8 189.5 %all-to-all-start.2 = ((bf16[16,512,256]{1,2,0:T(8,128)(2,1)}), bf16[16,512,256]{1,2,0:T(8,128)(2,1)}, u32[]{:S(2)}, u32[]{:S(2)}) async-start(bf16[16,512,256]{1,2,0:T(8,128)(2,1)} %stack.2), calls=%async_computation.3 | async-start | bytes 8388608 | tf_op jit(solution)/shard_map/all_to_all | solution.py:48
Sparse Core Ops, SparseCore 0:
  68.6 72.2 reduce-scatter.1
